TPU v7x, 128 devices: a whole 4x4x4 slice. The times are simulated.
128 devices in a mesh: fsdp: 16 (over x_hi, y, core), dp: 8 (over z, x_lo).
Axes of the slice: x: 4 (x_hi: 2, x_lo: 2; x = x_hi * 2 + x_lo), y: 4, z: 4, core: 2. Of those that a mesh axis runs over, the one named last changes fastest.
Arguments:
- hidden: bfloat16 [12288, 8192], P('fsdp', 'dp'), may hold values from -6 to 6
- combine_weight: float32 [12288], P('fsdp'), may hold values from 0.2 to 1
- down_weight: bfloat16 [4096, 2, 8192], P('fsdp', None, 'dp'), may hold values from -0.0625 to 0.0625
- cotangent: bfloat16 [12288, 4096], P('fsdp', 'dp'), may hold values from -6 to 6
- expert_rows: int32 [16, 2], P('fsdp'), may hold values from 1 to 640, as said below
- block_expert: int32 [96], P('fsdp'), may hold values from 0 to 1, as said below
- slot_token: int32 [12288], P('fsdp'), may hold values from 0 to 767, as said below
Outputs:
- expert_out: bfloat16 [12288, 4096], P('fsdp', 'dp')
- grad_hidden: bfloat16 [12288, 8192], P('fsdp', 'dp')
- grad_down: bfloat16 [4096, 2, 8192], P('fsdp', None, 'dp')
Inputs may be any that keep to these rules, and one draw needn't show every extreme that they name: `expert_rows`: row i gives the live rows of the first and the second expert in group i; the first expert's rows fill blocks from block 0 on, the second's start at the next free block, each takes ceil(rows / 128) blocks and both together at most 6; in every draw some group uses all 6 blocks. `block_expert`: within each group: 0 for the first expert's blocks, 1 for every later block; blocks past both experts' have no live rows. `slot_token`: tokens counted within the slot's group; the live slots of one expert in a group name different tokens of that group; slots that are not live hold arbitrary tokens.
All inputs are finite; a program needn't handle non-finite values.
Results may differ from a plain program's by a relative error of at most 0.014.
Values may be sent and summed in bfloat16 or wider, within the bound.
No kernel may reach another device: no remote copies, remote signals or barrier semaphores. Data moves between devices by JAX's collectives and lax.ppermute only.
A program may use at most 192 MiB of HBM per device.

v0:
```python
import math
import jax
import jax.numpy as jnp
from jax import lax
from jax.sharding import PartitionSpec as P

EXPERTS = 2
BLK = 128


def local(hidden, combine_weight, down_weight, cotangent, expert_rows, block_expert, slot_token):
    slot_count = hidden.shape[0]
    hidden_width = hidden.shape[1]
    block_count = block_expert.shape[0]
    positions = jnp.arange(slot_count, dtype=jnp.int32)
    blocks = positions // BLK
    live_rows = expert_rows[0]
    first_blocks = (live_rows[0] + BLK - 1) // BLK
    second_blocks = (live_rows[1] + BLK - 1) // BLK
    live = jnp.where(
        blocks < first_blocks,
        positions < live_rows[0],
        (blocks < first_blocks + second_blocks) & (positions - first_blocks * BLK < live_rows[1]),
    )
    slot_scale = combine_weight * live.astype(jnp.float32)
    full_cot = lax.all_gather(cotangent, "dp", axis=1, tiled=True)
    model_width = full_cot.shape[1]
    slot_cot = (slot_scale[:, None] * full_cot[slot_token].astype(jnp.float32)).astype(jnp.bfloat16)
    hid_blocks = hidden.reshape(block_count, BLK, hidden_width)
    cot_blocks = slot_cot.reshape(block_count, BLK, model_width)
    panel = lax.all_gather(down_weight, "fsdp", axis=0, tiled=True)
    extent = panel.shape[0]

    def per_block(carry, inputs):
        hid_block, cot_block, expert = inputs
        weight = lax.dynamic_index_in_dim(panel, expert, 1, keepdims=False)
        out_block = jnp.einsum("th,ch->tc", hid_block, weight, preferred_element_type=jnp.float32)
        grad_block = jnp.einsum("tc,ch->th", cot_block, weight, preferred_element_type=jnp.float32)
        return (carry, (out_block, grad_block))

    unused, (out_piece, grad_piece) = lax.scan(per_block, 0, (hid_blocks, cot_blocks, block_expert))
    slot_out = out_piece.reshape(slot_count, extent)
    slot_out, hidden_grad = (slot_out, grad_piece.reshape(slot_count, hidden_width))
    token_count = cotangent.shape[0]
    combined = (
        jnp.zeros((token_count, model_width), jnp.float32)
        .at[slot_token]
        .add(slot_scale[:, None] * slot_out)
    )
    expert_out = lax.psum_scatter(
        combined.astype(jnp.bfloat16), "dp", scatter_dimension=1, tiled=True
    )
    block_marks = (block_expert[:, None] == jnp.arange(EXPERTS, dtype=jnp.int32)[None, :]).astype(
        jnp.bfloat16
    )
    slot_marks = jnp.repeat(block_marks, BLK, axis=0)
    masked = slot_marks[:, :, None] * slot_cot[:, None, :]
    summed = lax.psum_scatter(
        jnp.einsum("sec,sh->ceh", masked, hidden, preferred_element_type=jnp.float32).astype(
            jnp.bfloat16
        ),
        "fsdp",
        scatter_dimension=0,
        tiled=True,
    ).astype(jnp.float32)
    grad_scale = 1.0 / math.sqrt(lax.axis_size("fsdp") * slot_count)
    grad_down = (summed * grad_scale).astype(jnp.bfloat16)
    return (expert_out, hidden_grad.astype(jnp.bfloat16), grad_down)


def solution(mesh):
    in_specs = (
        P("fsdp", "dp"),
        P("fsdp"),
        P("fsdp", None, "dp"),
        P("fsdp", "dp"),
        P("fsdp", None),
        P("fsdp"),
        P("fsdp"),
    )
    out_specs = (P("fsdp", "dp"), P("fsdp", "dp"), P("fsdp", None, "dp"))
    return jax.shard_map(local, mesh=mesh, in_specs=in_specs, out_specs=out_specs, check_vma=False)
```

profile of v0, /device:TPU:1, one launch (start us, length us, event | category | flops | bytes accessed | tf_op | source)
XLA Modules:
  0.0 673.4 jit_solution(6814083249735016535)
XLA Ops:
  18.3 123.9 %all-gather.5.cloned.1.call-done = bf16[768,4096]{1,0:T(8,128)(2,1)} async-done(((bf16[768,512]{1,0:T(8,128)(2,1)}), bf16[768,4096]{1,0:T(8,128)(2,1)}) %all-gather.5.cloned.1.call-update) | async-done | bytes 6291472 | tf_op jit(solution)/shard_map/all_gather | solution.py:26
  142.2 15.6 %gather_fusion = bf16[768,4096]{1,0:T(8,128)(2,1)} fusion(bf16[768,4096]{1,0:T(8,128)(2,1)} %all-gather.5.cloned.1.call-done, s32[1024]{0:T(1024)S(1)} %pad_clamp_fusion), kind=kCustom, calls=%fused_computation | custom fusion | bytes 12585984 | tf_op jit(solution)/shard_map/gather | solution.py:28
  157.8 8.0 %multiply_convert_fusion.1 = bf16[6,128,4096]{2,1,0:T(8,128)(2,1)} fusion(f32[6,128]{1,0:T(8,128)S(1)} %fusion.42, bf16[6,128,4096]{2,1,0:T(8,128)(2,1)} %bitcast.64), kind=kLoop, calls=%fused_computation.23 | loop fusion | flops 9437184 | bytes 12585984 | tf_op jit(solution)/shard_map/convert_element_type | solution.py:28
  165.7 89.9 %all-gather.3.cloned.1.call-done = bf16[4096,2,1024]{2,0,1:T(8,128)(2,1)} async-done(((bf16[256,2,1024]{2,0,1:T(8,128)(2,1)}), bf16[4096,2,1024]{2,0,1:T(8,128)(2,1)}) %all-gather.3.cloned.1.call-update) | async-done | bytes 16777232 | tf_op jit(solution)/shard_map/all_gather | solution.py:31
  255.6 94.9 %while.12 = (s32[]{:T(128)}, f32[6,128,4096]{2,1,0:T(8,128)}, bf16[6,128,1024]{2,1,0:T(8,128)(2,1)}, bf16[6,128,1024]{2,1,0:T(8,128)(2,1)S(1)}, s32[6]{0:T(128)S...) while((s32[]{:T(128)}, f32[6,128,4096]{2,1,0:T(8,128)}, ...), condition=%wide.region_1.2_spmd, body=%wide.region_0.1_spmd.sunk | while | flops 2147483648 | bytes 20711580 | solution.py:41
  258.2 7.6 %fusion.53 = f32[6,128,4096]{2,1,0:T(8,128)} fusion(f32[6,128,4096]{2,1,0:T(8,128)} %get-tuple-element.121, s32[]{:T(128)} %get-tuple-element.120, bf16[4096,2,1024]{2,0,1:T(8,128)(2,1)} %get-tuple-element.135, s32[]{:T(128)S(6)} %select_n.50, bf16[6,128,1024]{2,1,0:T(8,128)(2,1)S(1)} %get-tuple-element.133), kind=kOutput, calls=%fused_computation.9.clone.1 | convolution fusion | flops 1073741824 | bytes 10748932 | tf_op jit(solution)/shard_map/while/body/eval_jaxpr/th,ch->tc/dot_general | solution.py:37
  265.8 5.7 fusion.54
  274.0 7.6 %fusion.53 = f32[6,128,4096]{2,1,0:T(8,128)} fusion(f32[6,128,4096]{2,1,0:T(8,128)} %get-tuple-element.121, s32[]{:T(128)} %get-tuple-element.120, bf16[4096,2,1024]{2,0,1:T(8,128)(2,1)} %get-tuple-element.135, s32[]{:T(128)S(6)} %select_n.50, bf16[6,128,1024]{2,1,0:T(8,128)(2,1)S(1)} %get-tuple-element.133), kind=kOutput, calls=%fused_computation.9.clone.1 | convolution fusion | flops 1073741824 | bytes 10748932 | tf_op jit(solution)/shard_map/while/body/eval_jaxpr/th,ch->tc/dot_general | solution.py:37
  281.5 5.7 fusion.54
  289.8 7.6 %fusion.53 = f32[6,128,4096]{2,1,0:T(8,128)} fusion(f32[6,128,4096]{2,1,0:T(8,128)} %get-tuple-element.121, s32[]{:T(128)} %get-tuple-element.120, bf16[4096,2,1024]{2,0,1:T(8,128)(2,1)} %get-tuple-element.135, s32[]{:T(128)S(6)} %select_n.50, bf16[6,128,1024]{2,1,0:T(8,128)(2,1)S(1)} %get-tuple-element.133), kind=kOutput, calls=%fused_computation.9.clone.1 | convolution fusion | flops 1073741824 | bytes 10748932 | tf_op jit(solution)/shard_map/while/body/eval_jaxpr/th,ch->tc/dot_general | solution.py:37
  297.4 5.7 fusion.54
  305.6 7.6 %fusion.53 = f32[6,128,4096]{2,1,0:T(8,128)} fusion(f32[6,128,4096]{2,1,0:T(8,128)} %get-tuple-element.121, s32[]{:T(128)} %get-tuple-element.120, bf16[4096,2,1024]{2,0,1:T(8,128)(2,1)} %get-tuple-element.135, s32[]{:T(128)S(6)} %select_n.50, bf16[6,128,1024]{2,1,0:T(8,128)(2,1)S(1)} %get-tuple-element.133), kind=kOutput, calls=%fused_computation.9.clone.1 | convolution fusion | flops 1073741824 | bytes 10748932 | tf_op jit(solution)/shard_map/while/body/eval_jaxpr/th,ch->tc/dot_general | solution.py:37
  313.2 5.7 fusion.54
  321.4 7.6 %fusion.53 = f32[6,128,4096]{2,1,0:T(8,128)} fusion(f32[6,128,4096]{2,1,0:T(8,128)} %get-tuple-element.121, s32[]{:T(128)} %get-tuple-element.120, bf16[4096,2,1024]{2,0,1:T(8,128)(2,1)} %get-tuple-element.135, s32[]{:T(128)S(6)} %select_n.50, bf16[6,128,1024]{2,1,0:T(8,128)(2,1)S(1)} %get-tuple-element.133), kind=kOutput, calls=%fused_computation.9.clone.1 | convolution fusion | flops 1073741824 | bytes 10748932 | tf_op jit(solution)/shard_map/while/body/eval_jaxpr/th,ch->tc/dot_general | solution.py:37
  329.0 5.7 fusion.54
  337.2 7.6 %fusion.53 = f32[6,128,4096]{2,1,0:T(8,128)} fusion(f32[6,128,4096]{2,1,0:T(8,128)} %get-tuple-element.121, s32[]{:T(128)} %get-tuple-element.120, bf16[4096,2,1024]{2,0,1:T(8,128)(2,1)} %get-tuple-element.135, s32[]{:T(128)S(6)} %select_n.50, bf16[6,128,1024]{2,1,0:T(8,128)(2,1)S(1)} %get-tuple-element.133), kind=kOutput, calls=%fused_computation.9.clone.1 | convolution fusion | flops 1073741824 | bytes 10748932 | tf_op jit(solution)/shard_map/while/body/eval_jaxpr/th,ch->tc/dot_general | solution.py:37
  344.8 5.7 fusion.54
  350.5 14.9 %multiply_convert_fusion = (bf16[768,4096]{1,0:T(8,128)(2,1)}, f32[768,4096]{1,0:T(8,128)}) fusion(f32[768]{0:T(1024)S(1)} %fusion.38, bf16[768,4096]{1,0:T(8,128)(2,1)} %gather_fusion, f32[6,128,4096]{2,1,0:T(8,128)} %get-tuple-element.41), kind=kLoop, calls=%fused_computation.22 | loop fusion | flops 12582912 | bytes 37751808 | tf_op jit(solution)/shard_map/convert_element_type | solution.py:28
  365.5 8.7 %copy.13 = bf16[768,4096]{0,1:T(8,128)(2,1)} copy(bf16[768,4096]{1,0:T(8,128)(2,1)} %get-tuple-element.63) | data formatting | bytes 12582912 | tf_op jit(solution)/shard_map/convert_element_type | solution.py:28
  374.1 17.7 %convert_bitcast_fusion = bf16[4096,2,1024]{2,0,1:T(8,128)(2,1)} fusion(bf16[768,4096]{0,1:T(8,128)(2,1)} %copy.13, bf16[768,2]{0,1:T(2,128)(2,1)S(1)} %bitcast.65, bf16[768,1024]{1,0:T(8,128)(2,1)S(1)} %bitcast.67), kind=kOutput, calls=%fused_computation.18 | convolution fusion | flops 12899581952 | bytes 24644608 | tf_op jit(solution)/shard_map/sec,sh->ceh/dot_general | solution.py:59
  391.9 32.3 %scatter_custom_fusion = f32[768,4096]{1,0:T(8,128)} fusion(s32[768]{0:T(1024)S(1)} %compare_select_fusion, f32[768,4096]{1,0:T(8,128)} %get-tuple-element.64, f32[]{:T(128)} %constant.60.clone.1), kind=kCustom, calls=%fused_computation.26 | custom fusion | flops 3145728 | bytes 12583424 | tf_op jit(solution)/shard_map/scatter-add | solution.py:48
  424.2 8.4 %convert_element_type.51 = bf16[768,4096]{1,0:T(8,128)(2,1)} convert(f32[768,4096]{1,0:T(8,128)} %scatter_custom_fusion) | non-fusion elementwise | flops 3145728 | bytes 18874368 | tf_op jit(solution)/shard_map/convert_element_type | solution.py:51
  432.6 103.0 %reduce-scatter.5.cloned.1.call-done = bf16[256,2,1024]{2,0,1:T(8,128)(2,1)} async-done(((bf16[4096,2,1024]{2,0,1:T(8,128)(2,1)}), bf16[256,2,1024]{2,0,1:T(8,128)(2,1)}) %reduce-scatter.5.cloned.1.call-update) | async-done | bytes 1048592 | tf_op jit(solution)/shard_map/reduce_scatter | solution.py:58
  539.0 127.8 %reduce-scatter.3.cloned.1.call-done = bf16[768,512]{1,0:T(8,128)(2,1)} async-done(((bf16[768,4096]{1,0:T(8,128)(2,1)}), bf16[768,512]{1,0:T(8,128)(2,1)}) %reduce-scatter.3.cloned.1.call-update) | async-done | bytes 786448 | tf_op jit(solution)/shard_map/reduce_scatter | solution.py:50
  (31 shorter events, 16.8 us)
Async XLA Ops:
  7.2 135.0 %all-gather.5.cloned.1.call-start = ((), (), s32[]{:S(2)}) async-start(), calls=%async_computation.3 | async-start | bytes 7077888 | tf_op jit(solution)/shard_map/all_gather | solution.py:26
  7.9 247.7 %all-gather.3.cloned.1.call-start = ((), (), s32[]{:S(2)}) async-start(), calls=%async_computation.2 | async-start | bytes 17825792 | tf_op jit(solution)/shard_map/all_gather | solution.py:31
  10.4 525.1 %reduce-scatter.5.cloned.1.call-start = ((), (), s32[]{:S(2)}) async-start(), calls=%async_computation.5 | async-start | bytes 17825792 | tf_op jit(solution)/shard_map/reduce_scatter | solution.py:58
  157.8 97.9 %copy-start = (bf16[768,1024]{1,0:T(8,128)(2,1)S(1)}, bf16[768,1024]{1,0:T(8,128)(2,1)}, u32[]{:S(2)}) copy-start(bf16[768,1024]{1,0:T(8,128)(2,1)} %param.9) | copy-start | bytes 4718596
  157.8 97.9 %copy-start.1 = (s32[6]{0:T(128)S(1)}, s32[6]{0:T(128)}, u32[]{:S(2)}) copy-start(s32[6]{0:T(128)} %param.14) | copy-start | bytes 76
  391.9 275.0 %reduce-scatter.3.cloned.1.call-start = ((), (), s32[]{:S(2)}) async-start(), calls=%async_computation.4 | async-start | bytes 7077888 | tf_op jit(solution)/shard_map/reduce_scatter | solution.py:50
Sparse Core Ops, SparseCore 0:
  9.6 132.4 all-gather.4
  145.3 110.3 all-gather.2
  392.0 143.4 reduce-scatter.4
  538.4 128.4 reduce-scatter.2
where the time goes:
time: 674 us; the launch traced here: 673 us
  waiting for transfers between devices  445 us (66%)
  matrix products  97.4 us (14%)
  other arithmetic  70.1 us (10%)
  local copies, waits for them, and re-layouts  33.6 us (5%)
  between operations  15.1 us (2%)
  loops' own time  11.7 us (2%)
    reduce_scatter x1, waiting for transfers between devices, local(): lax.psum_scatter(combined.astype(jnp.bfloat16), 'dp', scatter_dimension=1...  128 us
    all_gather x1, waiting for transfers between devices, local(): full_cot = lax.all_gather(cotangent, 'dp', axis=1, tiled=True)  124 us
    reduce_scatter x1, waiting for transfers between devices, local(): lax.psum_scatter(jnp.einsum('sec,sh->ceh', masked, hidden, preferred_elem...  103 us
    all_gather x1, waiting for transfers between devices, local(): panel = lax.all_gather(down_weight, 'fsdp', axis=0, tiled=True)  89.9 us
    dot_general x6, matrix products, per_block(): jnp.einsum('th,ch->tc', hid_block, weight, preferred_element_type=jnp.flo...  45.6 us
    dot_general x6, matrix products, per_block(): jnp.einsum('tc,ch->th', cot_block, weight, preferred_element_type=jnp.flo...  34.1 us
    scatter-add x1, other arithmetic, local(): combined = jnp.zeros((token_count, model_width), jnp.float32).at[slot_tok...  32.3 us
    convert_element_type x2, other arithmetic, local(): (slot_scale[:, None] * full_cot[slot_token].astype(jnp.float32)).astype(j...  22.9 us
  transfers between devices with their start and end apart: 4, of which 4 were waited for; matrix products, arithmetic and copies ran while one was open for 11% of the time, Pallas kernels for 0%

commit v1 on v0

--- a/solution.py
+++ b/solution.py
@@ -23,7 +23,9 @@
         (blocks < first_blocks + second_blocks) & (positions - first_blocks * BLK < live_rows[1]),
     )
     slot_scale = combine_weight * live.astype(jnp.float32)
-    full_cot = lax.all_gather(cotangent, "dp", axis=1, tiled=True)
+    full_cot = jnp.concatenate(
+        lax.all_to_all(jnp.stack([cotangent] * lax.axis_size("dp")), "dp", 0, 0), axis=1
+    )
     model_width = full_cot.shape[1]
     slot_cot = (slot_scale[:, None] * full_cot[slot_token].astype(jnp.float32)).astype(jnp.bfloat16)
     hid_blocks = hidden.reshape(block_count, BLK, hidden_width)

time: 674 us -> 588 us (0.87)
  waiting for transfers between devices: 445 us -> 345 us
  local copies, waits for them, and re-layouts: 33.6 us -> 43.5 us
  starting transfers between devices: 0.16 us -> 6.91 us
    all_gather x1 -> x0, waiting for transfers between devices: 124 us -> none  [local(): full_cot = lax.all_gather(cotangent, 'dp', axis=1, tiled=True)]
    all_to_all x0 -> x1, waiting for transfers between devices: none -> 107 us  [local(): lax.all_to_all(jnp.stack([cotangent] * lax.axis_size('dp')), 'dp', 0, 0)]
    all_gather x1, waiting for transfers between devices: 89.9 us -> 4.23 us  [local(): panel = lax.all_gather(down_weight, 'fsdp', axis=0, tiled=True)]
    all_to_all x0 -> x1, starting transfers between devices: none -> 6.79 us  [local(): lax.all_to_all(jnp.stack([cotangent] * lax.axis_size('dp')), 'dp', 0, 0)]
  transfers between devices with their start and end apart: 4 -> 4, of which waited for: 4 -> 4; matrix products, arithmetic and copies ran while one was open for 11% -> 14% of each run, Pallas kernels for 0% -> 0%
where the time goes in v1:
time: 588 us; the launch traced here: 587 us
  waiting for transfers between devices  345 us (59%)
  matrix products  97.3 us (17%)
  other arithmetic  67.6 us (11%)
  local copies, waits for them, and re-layouts  43.5 us (7%)
  between operations  15.2 us (3%)
  loops' own time  11.7 us (2%)
  starting transfers between devices  6.91 us (1%)
    reduce_scatter x1, waiting for transfers between devices, local(): lax.psum_scatter(combined.astype(jnp.bfloat16), 'dp', scatter_dimension=1...  128 us
    all_to_all x1, waiting for transfers between devices, local(): lax.all_to_all(jnp.stack([cotangent] * lax.axis_size('dp')), 'dp', 0, 0)  107 us
    reduce_scatter x1, waiting for transfers between devices, local(): lax.psum_scatter(jnp.einsum('sec,sh->ceh', masked, hidden, preferred_elem...  105 us
    dot_general x6, matrix products, per_block(): jnp.einsum('th,ch->tc', hid_block, weight, preferred_element_type=jnp.flo...  45.5 us
    dot_general x6, matrix products, per_block(): jnp.einsum('tc,ch->th', cot_block, weight, preferred_element_type=jnp.flo...  34.1 us
    scatter-add x1, other arithmetic, local(): combined = jnp.zeros((token_count, model_width), jnp.float32).at[slot_tok...  32.6 us
    convert_element_type x2, other arithmetic, local(): (slot_scale[:, None] * full_cot[slot_token].astype(jnp.float32)).astype(j...  22.8 us
    dot_general x1, matrix products, local(): jnp.einsum('sec,sh->ceh', masked, hidden, preferred_element_type=jnp.floa...  17.7 us
  transfers between devices with their start and end apart: 4, of which 4 were waited for; matrix products, arithmetic and copies ran while one was open for 14% of the time, Pallas kernels for 0%

profile of v1, /device:TPU:1, one launch (start us, length us, event | category | flops | bytes accessed | tf_op | source)
XLA Modules:
  0.0 587.0 jit_solution(4173383082600168386)
XLA Ops:
  14.0 6.8 %all-to-all-start = ((bf16[8,768,512]{2,1,0:T(8,128)(2,1)}), bf16[8,768,512]{2,1,0:T(8,128)(2,1)}, u32[]{:S(2)}, u32[]{:S(2)}) async-start(bf16[8,768,512]{2,1,0:T(8,128)(2,1)} %stack.2), calls=%async_computation | async-start | bytes 12582912 | tf_op jit(solution)/shard_map/all_to_all | solution.py:27
  25.6 107.0 %all-to-all-done = bf16[8,768,512]{2,1,0:T(8,128)(2,1)} async-done(((bf16[8,768,512]{2,1,0:T(8,128)(2,1)}), bf16[8,768,512]{2,1,0:T(8,128)(2,1)}, u32[]{:S(2)}, u32[]{:S(2)}) %all-to-all-start) | async-done | bytes 6291488 | tf_op jit(solution)/shard_map/all_to_all | solution.py:27
  132.6 6.3 %copy.19 = bf16[8,96,8,512]{3,2,0,1:T(8,128)(2,1)} copy(bf16[8,96,8,512]{3,2,1,0:T(8,128)(2,1)} %bitcast.16) | data formatting | bytes 12582912 | tf_op jit(solution)/shard_map/reshape | solution.py:26
  138.9 15.6 %gather_fusion = bf16[768,4096]{1,0:T(8,128)(2,1)} fusion(bf16[768,4096]{1,0:T(8,128)(2,1)} %bitcast.67, s32[1024]{0:T(1024)S(1)} %pad_clamp_fusion), kind=kCustom, calls=%fused_computation | custom fusion | bytes 12585984 | tf_op jit(solution)/shard_map/gather | solution.py:30
  154.5 8.1 %multiply_convert_fusion.1 = bf16[6,128,4096]{2,1,0:T(8,128)(2,1)} fusion(f32[6,128]{1,0:T(8,128)S(1)} %fusion.42, bf16[6,128,4096]{2,1,0:T(8,128)(2,1)} %bitcast.68), kind=kLoop, calls=%fused_computation.23 | loop fusion | flops 9437184 | bytes 12585984 | tf_op jit(solution)/shard_map/convert_element_type | solution.py:30
  166.8 94.7 %while.12 = (s32[]{:T(128)}, f32[6,128,4096]{2,1,0:T(8,128)}, bf16[6,128,1024]{2,1,0:T(8,128)(2,1)}, bf16[6,128,1024]{2,1,0:T(8,128)(2,1)S(1)}, s32[6]{0:T(128)S...) while((s32[]{:T(128)}, f32[6,128,4096]{2,1,0:T(8,128)}, ...), condition=%wide.region_1.2_spmd, body=%wide.region_0.1_spmd.sunk | while | flops 2147483648 | bytes 20711580 | solution.py:43
  169.3 7.6 %fusion.53 = f32[6,128,4096]{2,1,0:T(8,128)} fusion(f32[6,128,4096]{2,1,0:T(8,128)} %get-tuple-element.124, s32[]{:T(128)} %get-tuple-element.123, bf16[4096,2,1024]{2,0,1:T(8,128)(2,1)} %get-tuple-element.138, s32[]{:T(128)S(6)} %select_n.50, bf16[6,128,1024]{2,1,0:T(8,128)(2,1)S(1)} %get-tuple-element.136), kind=kOutput, calls=%fused_computation.9.clone.1 | convolution fusion | flops 1073741824 | bytes 10748932 | tf_op jit(solution)/shard_map/while/body/eval_jaxpr/th,ch->tc/dot_general | solution.py:39
  176.9 5.7 fusion.54
  185.1 7.6 %fusion.53 = f32[6,128,4096]{2,1,0:T(8,128)} fusion(f32[6,128,4096]{2,1,0:T(8,128)} %get-tuple-element.124, s32[]{:T(128)} %get-tuple-element.123, bf16[4096,2,1024]{2,0,1:T(8,128)(2,1)} %get-tuple-element.138, s32[]{:T(128)S(6)} %select_n.50, bf16[6,128,1024]{2,1,0:T(8,128)(2,1)S(1)} %get-tuple-element.136), kind=kOutput, calls=%fused_computation.9.clone.1 | convolution fusion | flops 1073741824 | bytes 10748932 | tf_op jit(solution)/shard_map/while/body/eval_jaxpr/th,ch->tc/dot_general | solution.py:39
  200.8 7.6 %fusion.53 = f32[6,128,4096]{2,1,0:T(8,128)} fusion(f32[6,128,4096]{2,1,0:T(8,128)} %get-tuple-element.124, s32[]{:T(128)} %get-tuple-element.123, bf16[4096,2,1024]{2,0,1:T(8,128)(2,1)} %get-tuple-element.138, s32[]{:T(128)S(6)} %select_n.50, bf16[6,128,1024]{2,1,0:T(8,128)(2,1)S(1)} %get-tuple-element.136), kind=kOutput, calls=%fused_computation.9.clone.1 | convolution fusion | flops 1073741824 | bytes 10748932 | tf_op jit(solution)/shard_map/while/body/eval_jaxpr/th,ch->tc/dot_general | solution.py:39
  208.4 5.7 fusion.54
  216.6 7.6 %fusion.53 = f32[6,128,4096]{2,1,0:T(8,128)} fusion(f32[6,128,4096]{2,1,0:T(8,128)} %get-tuple-element.124, s32[]{:T(128)} %get-tuple-element.123, bf16[4096,2,1024]{2,0,1:T(8,128)(2,1)} %get-tuple-element.138, s32[]{:T(128)S(6)} %select_n.50, bf16[6,128,1024]{2,1,0:T(8,128)(2,1)S(1)} %get-tuple-element.136), kind=kOutput, calls=%fused_computation.9.clone.1 | convolution fusion | flops 1073741824 | bytes 10748932 | tf_op jit(solution)/shard_map/while/body/eval_jaxpr/th,ch->tc/dot_general | solution.py:39
  224.2 5.7 fusion.54
  232.4 7.6 %fusion.53 = f32[6,128,4096]{2,1,0:T(8,128)} fusion(f32[6,128,4096]{2,1,0:T(8,128)} %get-tuple-element.124, s32[]{:T(128)} %get-tuple-element.123, bf16[4096,2,1024]{2,0,1:T(8,128)(2,1)} %get-tuple-element.138, s32[]{:T(128)S(6)} %select_n.50, bf16[6,128,1024]{2,1,0:T(8,128)(2,1)S(1)} %get-tuple-element.136), kind=kOutput, calls=%fused_computation.9.clone.1 | convolution fusion | flops 1073741824 | bytes 10748932 | tf_op jit(solution)/shard_map/while/body/eval_jaxpr/th,ch->tc/dot_general | solution.py:39
  240.0 5.7 fusion.54
  248.2 7.6 %fusion.53 = f32[6,128,4096]{2,1,0:T(8,128)} fusion(f32[6,128,4096]{2,1,0:T(8,128)} %get-tuple-element.124, s32[]{:T(128)} %get-tuple-element.123, bf16[4096,2,1024]{2,0,1:T(8,128)(2,1)} %get-tuple-element.138, s32[]{:T(128)S(6)} %select_n.50, bf16[6,128,1024]{2,1,0:T(8,128)(2,1)S(1)} %get-tuple-element.136), kind=kOutput, calls=%fused_computation.9.clone.1 | convolution fusion | flops 1073741824 | bytes 10748932 | tf_op jit(solution)/shard_map/while/body/eval_jaxpr/th,ch->tc/dot_general | solution.py:39
  255.8 5.7 fusion.54
  261.5 14.8 %multiply_convert_fusion = (bf16[768,4096]{1,0:T(8,128)(2,1)}, f32[768,4096]{1,0:T(8,128)}) fusion(f32[768]{0:T(1024)S(1)} %fusion.38, bf16[768,4096]{1,0:T(8,128)(2,1)} %gather_fusion, f32[6,128,4096]{2,1,0:T(8,128)} %get-tuple-element.41), kind=kLoop, calls=%fused_computation.22 | loop fusion | flops 12582912 | bytes 37751808 | tf_op jit(solution)/shard_map/convert_element_type | solution.py:30
  276.2 8.6 %copy.17 = bf16[768,4096]{0,1:T(8,128)(2,1)} copy(bf16[768,4096]{1,0:T(8,128)(2,1)} %get-tuple-element.66) | data formatting | bytes 12582912 | tf_op jit(solution)/shard_map/convert_element_type | solution.py:30
  284.9 17.7 %convert_bitcast_fusion = bf16[4096,2,1024]{2,0,1:T(8,128)(2,1)} fusion(bf16[768,4096]{0,1:T(8,128)(2,1)} %copy.17, bf16[768,2]{0,1:T(2,128)(2,1)S(1)} %bitcast.69, bf16[768,1024]{1,0:T(8,128)(2,1)S(1)} %bitcast.71), kind=kOutput, calls=%fused_computation.18 | convolution fusion | flops 12899581952 | bytes 24644608 | tf_op jit(solution)/shard_map/sec,sh->ceh/dot_general | solution.py:61
  302.7 32.6 %scatter_custom_fusion = f32[768,4096]{1,0:T(8,128)} fusion(s32[768]{0:T(1024)S(1)} %compare_select_fusion, f32[768,4096]{1,0:T(8,128)} %get-tuple-element.67, f32[]{:T(128)} %constant.60.clone.1), kind=kCustom, calls=%fused_computation.26 | custom fusion | flops 3145728 | bytes 12583424 | tf_op jit(solution)/shard_map/scatter-add | solution.py:50
  335.3 8.2 %convert_element_type.51 = bf16[768,4096]{1,0:T(8,128)(2,1)} convert(f32[768,4096]{1,0:T(8,128)} %scatter_custom_fusion) | non-fusion elementwise | flops 3145728 | bytes 18874368 | tf_op jit(solution)/shard_map/convert_element_type | solution.py:53
  343.5 105.4 %reduce-scatter.5.cloned.1.call-done = bf16[256,2,1024]{2,0,1:T(8,128)(2,1)} async-done(((bf16[4096,2,1024]{2,0,1:T(8,128)(2,1)}), bf16[256,2,1024]{2,0,1:T(8,128)(2,1)}) %reduce-scatter.5.cloned.1.call-update) | async-done | bytes 1048592 | tf_op jit(solution)/shard_map/reduce_scatter | solution.py:60
  452.4 128.0 %reduce-scatter.3.cloned.1.call-done = bf16[768,512]{1,0:T(8,128)(2,1)} async-done(((bf16[768,4096]{1,0:T(8,128)(2,1)}), bf16[768,512]{1,0:T(8,128)(2,1)}) %reduce-scatter.3.cloned.1.call-update) | async-done | bytes 786448 | tf_op jit(solution)/shard_map/reduce_scatter | solution.py:52
  (38 shorter events, 27.1 us)
Async XLA Ops:
  7.2 159.6 %all-gather.2.cloned.1.call-start = ((), (), s32[]{:S(2)}) async-start(), calls=%async_computation.3 | async-start | bytes 17825792 | tf_op jit(solution)/shard_map/all_gather | solution.py:33
  9.7 11.2 %copy-start.2 = (s32[1,2]{1,0:T(1,128)S(1)}, s32[1,2]{1,0:T(1,128)}, u32[]{:S(2)}) copy-start(s32[1,2]{1,0:T(1,128)} %param.13) | copy-start | bytes 28
  9.7 13.1 %copy-start.4 = (s32[6]{0:T(128)S(1)}, s32[6]{0:T(128)}, u32[]{:S(2)}) copy-start(s32[6]{0:T(128)} %param.14) | copy-start | bytes 76
  9.7 13.2 %copy-start.1 = (s32[768]{0:T(1024)S(1)}, s32[768]{0:T(1024)}, u32[]{:S(2)}) copy-start(s32[768]{0:T(1024)} %param.15) | copy-start | bytes 9220
  9.7 13.2 %copy-start = (f32[768]{0:T(1024)S(1)}, f32[768]{0:T(1024)}, u32[]{:S(2)}) copy-start(f32[768]{0:T(1024)} %param.10) | copy-start | bytes 9220
  14.0 118.6 %all-to-all-start = ((bf16[8,768,512]{2,1,0:T(8,128)(2,1)}), bf16[8,768,512]{2,1,0:T(8,128)(2,1)}, u32[]{:S(2)}, u32[]{:S(2)}) async-start(bf16[8,768,512]{2,1,0:T(8,128)(2,1)} %stack.2), calls=%async_computation | async-start | bytes 12582912 | tf_op jit(solution)/shard_map/all_to_all | solution.py:27
  20.8 428.1 %reduce-scatter.5.cloned.1.call-start = ((), (), s32[]{:S(2)}) async-start(), calls=%async_computation.5 | async-start | bytes 17825792 | tf_op jit(solution)/shard_map/reduce_scatter | solution.py:60
  154.5 12.3 %copy-start.3 = (bf16[768,1024]{1,0:T(8,128)(2,1)S(1)}, bf16[768,1024]{1,0:T(8,128)(2,1)}, u32[]{:S(2)}) copy-start(bf16[768,1024]{1,0:T(8,128)(2,1)} %param.9) | copy-start | bytes 4718596
  302.6 277.8 %reduce-scatter.3.cloned.1.call-start = ((), (), s32[]{:S(2)}) async-start(), calls=%async_computation.4 | async-start | bytes 7077888 | tf_op jit(solution)/shard_map/reduce_scatter | solution.py:52
Sparse Core Ops, SparseCore 0:
  11.1 155.6 all-gather.1
  302.8 146.0 reduce-scatter.4
  451.9 128.4 reduce-scatter.2
